TPU v7x, 512 devices: a whole 4x4x16 slice. The times are simulated.
512 devices in a mesh: band: 32 (over x, z_lo), grid: 16 (over z_hi, y, core).
Axes of the slice: x: 4, y: 4, z: 16 (z_hi: 2, z_lo: 8; z = z_hi * 8 + z_lo), core: 2. Of those that a mesh axis runs over, the one named last changes fastest.
Arguments:
- trial_bands: float32 [64, 160, 32, 128], P('band', 'grid'), may hold values from -6 to 6
- potential: float32 [160, 32, 128], P('grid'), may hold values from -2 to 0
Outputs:
- filtered: float32 [64, 160, 32, 128], P('band', 'grid')
- projected: float32 [64, 64], P('band')
- residual_norms: float32 [64], P('band')
All inputs are finite; a program needn't handle non-finite values.
Results may differ from a plain program's by a relative error of at most 0.00016.
Values sent between devices are 32-bit elements; how exact they have to be, the bound alone decides.
No kernel may reach another device: no remote copies, remote signals or barrier semaphores. Data moves between devices by JAX's collectives and lax.ppermute only.
A program may use at most 64 MiB of HBM per device.

v0:
```python
import jax
import jax.numpy as jnp
from jax import lax
from jax.sharding import PartitionSpec as P

CENTER = 4.25
HALF_WIDTH = 3.75
LOWEST = -2.0
SIGMA_ONE = HALF_WIDTH / (LOWEST - CENTER)
FOUR_THIRDS = 4.0 / 3.0
TWELFTH = 1.0 / 12.0
filter_degree = 4


def padded_2(cells, sides, width):
    for axis, dim in sides:
        count = lax.axis_size(axis)
        head = lax.slice_in_dim(cells, 0, width, axis=dim)
        tail = lax.slice_in_dim(cells, cells.shape[dim] - width, cells.shape[dim], axis=dim)
        cells = jnp.concatenate(
            [
                lax.ppermute(tail, axis, [(i, (i + 1) % count) for i in range(count)]),
                cells,
                lax.ppermute(head, axis, [((i + 1) % count, i) for i in range(count)]),
            ],
            axis=dim,
        )
    return cells


def operate(field_in, potential):
    padded = padded_2(field_in, (("grid", 1),), 2)
    plane_count = field_in.shape[1]
    near_sum = padded[:, 1 : 1 + plane_count] + padded[:, 3 : 3 + plane_count]
    near_sum = near_sum + jnp.roll(field_in, 1, 2) + jnp.roll(field_in, -1, 2)
    near_sum = near_sum + jnp.roll(field_in, 1, 3) + jnp.roll(field_in, -1, 3)
    far_sum = padded[:, 0:plane_count] + padded[:, 4 : 4 + plane_count]
    far_sum = far_sum + jnp.roll(field_in, 2, 2) + jnp.roll(field_in, -2, 2)
    far_sum = far_sum + jnp.roll(field_in, 2, 3) + jnp.roll(field_in, -2, 3)
    kinetic = 0.5 * (7.5 * field_in - FOUR_THIRDS * near_sum + TWELFTH * far_sum)
    return kinetic + potential * field_in


def on_device(trial_bands, potential):
    sigma_now = SIGMA_ONE
    previous = trial_bands
    current = (operate(trial_bands, potential) - CENTER * trial_bands) * (SIGMA_ONE / HALF_WIDTH)
    for repeat_index in range(filter_degree - 1):
        sigma_next = 1.0 / (2.0 / SIGMA_ONE - sigma_now)
        following = (operate(current, potential) - CENTER * current) * (
            2.0 * sigma_next / HALF_WIDTH
        ) - sigma_now * sigma_next * previous
        previous, current, sigma_now = (current, following, sigma_next)
    applied = operate(current, potential)
    band_count = current.shape[0]
    flat_bands = current.reshape(band_count, -1)
    flat_image = applied.reshape(band_count, -1)
    cell_total = flat_bands.shape[1] * lax.axis_size("grid")
    inverse_cells = 1.0 / cell_total
    first_band = lax.axis_index("band") * band_count
    local_norms = jnp.sum(flat_image * flat_image, axis=1)
    panel_piece = lax.all_gather(current, "band", axis=0, tiled=True)
    flat_piece = panel_piece.reshape(panel_piece.shape[0], -1)
    margin_part = jnp.dot(
        flat_bands,
        flat_piece.T,
        precision=lax.Precision.HIGHEST,
        preferred_element_type=jnp.float32,
    )
    image_part = jnp.dot(
        flat_image,
        flat_piece.T,
        precision=lax.Precision.HIGHEST,
        preferred_element_type=jnp.float32,
    )
    margin_rows = margin_part
    image_rows = image_part
    margin_rows, image_rows, norm_rows = lax.psum((margin_rows, image_rows, local_norms), "grid")
    margin, subspace, image_norms = (
        lax.all_gather(margin_rows, "band", axis=0, tiled=True),
        lax.all_gather(image_rows, "band", axis=0, tiled=True),
        lax.all_gather(norm_rows, "band", axis=0, tiled=True),
    )
    margin = margin * inverse_cells
    subspace = subspace * inverse_cells
    image_norms = image_norms * inverse_cells
    factor = jnp.linalg.cholesky(margin)
    coefficients = lax.linalg.triangular_solve(factor, subspace.T, left_side=True, lower=True)
    projected = lax.linalg.triangular_solve(factor, coefficients.T, left_side=True, lower=True)
    residual_norms = image_norms - jnp.sum(coefficients * coefficients, axis=0)
    projected_rows = lax.dynamic_slice_in_dim(projected, first_band, band_count, 0)
    residual_rows = lax.dynamic_slice_in_dim(residual_norms, first_band, band_count, 0)
    return (current, projected_rows, residual_rows)


def solution(mesh):
    in_specs = (P("band", "grid", None, None), P("grid", None, None))
    out_specs = (P("band", "grid", None, None), P("band", None), P("band"))
    return jax.shard_map(
        on_device, mesh=mesh, in_specs=in_specs, out_specs=out_specs, check_vma=False
    )
```

profile of v0, /device:TPU:32, one launch (start us, length us, event | category | flops | bytes accessed | tf_op | source)
XLA Modules:
  0.0 828.4 jit_solution(4509007590177282399)
XLA Ops:
  7.2 0.9 fusion.157
  8.1 1.9 collective-permute-start
  10.0 16.7 %collective-permute-start.1 = (f32[2,2,32,128]{3,2,1,0:T(8,128)S(1)}, f32[2,2,32,128]{3,2,1,0:T(8,128)S(1)}, u32[]{:S(2)}, u32[]{:S(2)}) collective-permute-start(f32[2,2,32,128]{3,2,1,0:T(8,128)S(1)} %get-tuple-element.100), channel_id=1, source_target_pairs={{1,0},{2,1},{3,2},{4,3},{5,4},{6,5},{7,6},{8,7},{9,8},{10,9},{11,1... | collective-permute-start | bytes 196616 | tf_op jit(solution)/shard_map/ppermute | solution.py:24
  26.8 1.2 fusion.160
  28.0 1.2 fusion.161
  29.2 0.9 fusion.158
  30.2 1.2 fusion.159
  31.4 1.3 fusion.155
  32.6 1.2 fusion.156
  33.9 1.2 fusion.154
  35.0 0.9 broadcast_multiply_fusion.1
  36.0 0.9 fusion.153
  36.9 1.0 constant_dynamic-update-slice_fusion
  38.0 1.7 broadcast_multiply_fusion
  40.0 0.2 fusion.149
  40.4 0.2 fusion.145
  40.6 5.1 collective-permute-start.3
  45.7 1.9 collective-permute-start.2
  47.6 14.4 %collective-permute-done.2 = f32[2,2,32,128]{3,2,1,0:T(8,128)S(1)} collective-permute-done((f32[2,2,32,128]{3,2,1,0:T(8,128)S(1)}, f32[2,2,32,128]{3,2,1,0:T(8,128)S(1)}, u32[]{:S(2)}, u32[]{:S(2)}) %collective-permute-start.2) | collective-permute-done | bytes 65568 | tf_op jit(solution)/shard_map/ppermute | solution.py:22
  62.1 0.7 fusion.65
  62.9 0.2 fusion.139
  63.0 0.2 fusion.140
  63.5 0.2 fusion.136
  63.6 1.9 collective-permute-start.5
  65.5 2.4 collective-permute-start.4
  68.0 14.0 %collective-permute-done.4 = f32[2,2,32,128]{3,2,1,0:T(8,128)S(1)} collective-permute-done((f32[2,2,32,128]{3,2,1,0:T(8,128)S(1)}, f32[2,2,32,128]{3,2,1,0:T(8,128)S(1)}, u32[]{:S(2)}, u32[]{:S(2)}) %collective-permute-start.4) | collective-permute-done | bytes 65568 | tf_op jit(solution)/shard_map/ppermute | solution.py:22
  82.0 0.6 fusion.50
  82.7 0.2 fusion.130
  82.9 0.2 fusion.131
  83.3 0.2 fusion.127
  83.4 1.9 collective-permute-start.7
  85.4 2.4 collective-permute-start.6
  87.8 14.0 %collective-permute-done.6 = f32[2,2,32,128]{3,2,1,0:T(8,128)S(1)} collective-permute-done((f32[2,2,32,128]{3,2,1,0:T(8,128)S(1)}, f32[2,2,32,128]{3,2,1,0:T(8,128)S(1)}, u32[]{:S(2)}, u32[]{:S(2)}) %collective-permute-start.6) | collective-permute-done | bytes 65568 | tf_op jit(solution)/shard_map/ppermute | solution.py:22
  101.8 1.4 fusion.35
  103.2 1.3 dynamic-slice
  105.1 0.9 fusion.121
  106.0 1.9 collective-permute-start.9
  108.0 2.6 collective-permute-start.8
  110.6 0.9 fusion.122
  111.5 1.2 fusion.124
  112.7 1.2 fusion.125
  114.0 1.1 fusion.123
  115.1 1.2 fusion.119
  116.3 1.2 fusion.120
  117.6 1.1 fusion.118
  118.7 0.9 fusion.117
  119.7 4.7 collective-permute-done.8
  124.4 2.4 multiply_reduce_fusion
  126.8 241.7 %all-gather.4.cloned.1.call-done = f32[64,10,32,128]{3,2,1,0:T(8,128)} async-done(((f32[2,10,32,128]{3,2,1,0:T(8,128)}), f32[64,10,32,128]{3,2,1,0:T(8,128)}) %all-gather.4.cloned.1.call-update) | async-done | bytes 10485776 | tf_op jit(solution)/shard_map/all_gather | solution.py:62
  368.4 17.0 %fusion.4 = f32[2,64]{1,0:T(2,128)S(1)} fusion(f32[64,10,32,128]{3,2,1,0:T(8,128)} %all-gather.4.cloned.1.call-done, f32[2,10,32,128]{3,2,1,0:T(8,128)S(1)} %copy-done), kind=kOutput, calls=%fused_computation.4 | convolution fusion | flops 62914560 | bytes 10813952 | tf_op jit(solution)/shard_map/dot_general | solution.py:64
  385.5 12.8 %fusion.7 = f32[2,64]{1,0:T(2,128)S(1)} fusion(f32[64,10,32,128]{3,2,1,0:T(8,128)S(1)} %copy-done.2, f32[2,10,32,128]{3,2,1,0:T(8,128)S(1)} %get-tuple-element.14), kind=kOutput, calls=%fused_computation.5 | convolution fusion | flops 62914560 | bytes 10813952 | tf_op jit(solution)/shard_map/dot_general | solution.py:70
  398.3 62.3 %all-reduce.1 = (f32[2,64]{1,0:T(2,128)S(1)}, f32[2,64]{1,0:T(2,128)S(1)}, f32[2]{0:T(128)S(1)}) all-reduce(f32[2,64]{1,0:T(2,128)S(1)} %fusion.7, f32[2,64]{1,0:T(2,128)S(1)} %fusion.4, f32[2]{0:T(128)S(1)} %get-tuple-element.13), channel_id=1, replica_groups=mesh['band'=32,'grid'=16] {'grid'}, use_global_device_ids=true, to_apply=%region_3.4 | all-reduce | flops 258 | bytes 2064 | tf_op jit(solution)/shard_map/psum | solution.py:78
  460.6 115.9 %all-gather.1 = f32[32,2,64]{2,1,0:T(2,128)S(1)} all-gather(f32[1,2,64]{2,1,0:T(2,128)S(1)} %bitcast.38), channel_id=1, replica_groups=mesh['band'=32,'grid'=16] {'band'}, dimensions={0}, use_global_device_ids=true | all-gather | bytes 16896 | tf_op jit(solution)/shard_map/all_gather | solution.py:81
  576.5 117.9 %all-gather = f32[32,2,64]{2,1,0:T(2,128)S(1)} all-gather(f32[1,2,64]{2,1,0:T(2,128)S(1)} %bitcast.37), channel_id=1, replica_groups=mesh['band'=32,'grid'=16] {'band'}, dimensions={0}, use_global_device_ids=true | all-gather | bytes 16896 | tf_op jit(solution)/shard_map/all_gather | solution.py:80
  694.5 5.8 cholesky.18
  700.4 0.6 compare_reduce_fusion
  701.0 0.7 fusion.108
  701.7 4.9 custom-call.8
  706.6 0.3 multiply_reduce_fusion.1
  706.9 0.2 fusion.109
  707.1 0.2 dynamic-update-slice.3
  707.4 113.1 %all-reduce = f32[64]{0:T(128)S(1)} all-reduce(f32[64]{0:T(128)S(1)} %dynamic-update-slice.3), channel_id=1, replica_groups=mesh['band'=32,'grid'=16] {'band'}, use_global_device_ids=true, to_apply=%add | all-reduce | flops 64 | bytes 512
  820.4 0.6 constant_dynamic-slice_fusion
  821.0 0.6 dynamic_slice.7
  (44 shorter events, 1.4 us)
Async XLA Ops:
  7.2 361.3 %all-gather.4.cloned.1.call-start = ((), (), s32[]{:S(2)}) async-start(), calls=%async_computation | async-start | bytes 10813440 | tf_op jit(solution)/shard_map/all_gather | solution.py:62
  8.1 28.8 %collective-permute-start = (f32[2,2,32,128]{3,2,1,0:T(8,128)S(1)}, f32[2,2,32,128]{3,2,1,0:T(8,128)S(1)}, u32[]{:S(2)}, u32[]{:S(2)}) collective-permute-start(f32[2,2,32,128]{3,2,1,0:T(8,128)S(1)} %get-tuple-element.99), channel_id=1, source_target_pairs={{0,1},{1,2},{2,3},{3,4},{4,5},{5,6},{6,7},{7,8},{8,9},{9,10},{10,1... | collective-permute-start | bytes 196616 | tf_op jit(solution)/shard_map/ppermute | solution.py:22
  10.0 28.0 %collective-permute-start.1 = (f32[2,2,32,128]{3,2,1,0:T(8,128)S(1)}, f32[2,2,32,128]{3,2,1,0:T(8,128)S(1)}, u32[]{:S(2)}, u32[]{:S(2)}) collective-permute-start(f32[2,2,32,128]{3,2,1,0:T(8,128)S(1)} %get-tuple-element.100), channel_id=1, source_target_pairs={{1,0},{2,1},{3,2},{4,3},{5,4},{6,5},{7,6},{8,7},{9,8},{10,9},{11,1... | collective-permute-start | bytes 196616 | tf_op jit(solution)/shard_map/ppermute | solution.py:24
  31.3 30.8 %copy-start.1 = (f32[2,10,32,128]{3,2,1,0:T(8,128)S(1)}, f32[2,10,32,128]{3,2,1,0:T(8,128)}, u32[]{:S(2)}) copy-start(f32[2,10,32,128]{3,2,1,0:T(8,128)} %param.4) | copy-start | bytes 983044
  39.8 42.2 %copy-start.3 = (f32[10,32,128]{2,1,0:T(8,128)S(1)}, f32[10,32,128]{2,1,0:T(8,128)}, u32[]{:S(2)}) copy-start(f32[10,32,128]{2,1,0:T(8,128)} %param.5) | copy-start | bytes 491524
  40.6 7.1 collective-permute-start.3
  45.7 16.4 %collective-permute-start.2 = (f32[2,2,32,128]{3,2,1,0:T(8,128)S(1)}, f32[2,2,32,128]{3,2,1,0:T(8,128)S(1)}, u32[]{:S(2)}, u32[]{:S(2)}) collective-permute-start(f32[2,2,32,128]{3,2,1,0:T(8,128)S(1)} %get-tuple-element.87), channel_id=1, source_target_pairs={{0,1},{1,2},{2,3},{3,4},{4,5},{5,6},{6,7},{7,8},{8,9},{9,10},{10,1... | collective-permute-start | bytes 196616 | tf_op jit(solution)/shard_map/ppermute | solution.py:22
  63.6 4.4 collective-permute-start.5
  65.5 16.4 %collective-permute-start.4 = (f32[2,2,32,128]{3,2,1,0:T(8,128)S(1)}, f32[2,2,32,128]{3,2,1,0:T(8,128)S(1)}, u32[]{:S(2)}, u32[]{:S(2)}) collective-permute-start(f32[2,2,32,128]{3,2,1,0:T(8,128)S(1)} %get-tuple-element.69), channel_id=1, source_target_pairs={{0,1},{1,2},{2,3},{3,4},{4,5},{5,6},{6,7},{7,8},{8,9},{9,10},{10,1... | collective-permute-start | bytes 196616 | tf_op jit(solution)/shard_map/ppermute | solution.py:22
  83.4 4.4 collective-permute-start.7
  85.4 16.4 %collective-permute-start.6 = (f32[2,2,32,128]{3,2,1,0:T(8,128)S(1)}, f32[2,2,32,128]{3,2,1,0:T(8,128)S(1)}, u32[]{:S(2)}, u32[]{:S(2)}) collective-permute-start(f32[2,2,32,128]{3,2,1,0:T(8,128)S(1)} %get-tuple-element.51), channel_id=1, source_target_pairs={{0,1},{1,2},{2,3},{3,4},{4,5},{5,6},{6,7},{7,8},{8,9},{9,10},{10,1... | collective-permute-start | bytes 196616 | tf_op jit(solution)/shard_map/ppermute | solution.py:22
  103.2 265.3 %copy-start = (f32[2,10,32,128]{3,2,1,0:T(8,128)S(1)}, f32[2,10,32,128]{3,2,1,0:T(8,128)}, u32[]{:S(2)}) copy-start(f32[2,10,32,128]{3,2,1,0:T(8,128)} %fusion.35) | copy-start | bytes 983044
  106.0 13.6 %collective-permute-start.9 = (f32[2,2,32,128]{3,2,1,0:T(8,128)S(1)}, f32[2,2,32,128]{3,2,1,0:T(8,128)S(1)}, u32[]{:S(2)}, u32[]{:S(2)}) collective-permute-start(f32[2,2,32,128]{3,2,1,0:T(8,128)S(1)} %get-tuple-element.26), channel_id=1, source_target_pairs={{1,0},{2,1},{3,2},{4,3},{5,4},{6,5},{7,6},{8,7},{9,8},{10,9},{11,1... | collective-permute-start | bytes 196616 | tf_op jit(solution)/shard_map/ppermute | solution.py:24
  108.0 16.4 %collective-permute-start.8 = (f32[2,2,32,128]{3,2,1,0:T(8,128)S(1)}, f32[2,2,32,128]{3,2,1,0:T(8,128)S(1)}, u32[]{:S(2)}, u32[]{:S(2)}) collective-permute-start(f32[2,2,32,128]{3,2,1,0:T(8,128)S(1)} %get-tuple-element.25), channel_id=1, source_target_pairs={{0,1},{1,2},{2,3},{3,4},{4,5},{5,6},{6,7},{7,8},{8,9},{9,10},{10,1... | collective-permute-start | bytes 196616 | tf_op jit(solution)/shard_map/ppermute | solution.py:22
  368.4 17.0 %copy-start.2 = (f32[64,10,32,128]{3,2,1,0:T(8,128)S(1)}, f32[64,10,32,128]{3,2,1,0:T(8,128)}, u32[]{:S(2)}) copy-start(f32[64,10,32,128]{3,2,1,0:T(8,128)} %all-gather.4.cloned.1.call-done) | copy-start | bytes 31457284
Sparse Core Ops, SparseCore 0:
  103.3 265.0 all-gather.3
where the time goes:
time: 829 us; the launch traced here: 828 us
  blocking collectives  409 us (49%)
  waiting for transfers between devices  289 us (35%)
  starting transfers between devices  38.9 us (5%)
  matrix products  30.4 us (4%)
  local copies, waits for them, and re-layouts  26.3 us (3%)
  other arithmetic  19.9 us (2%)
  between operations  15.1 us (2%)
    all_gather x1, waiting for transfers between devices, on_device(): panel_piece = lax.all_gather(current, 'band', axis=0, tiled=True)  242 us
    all_gather x1, blocking collectives, on_device(): lax.all_gather(margin_rows, 'band', axis=0, tiled=True)  118 us
    all_gather x1, blocking collectives, on_device(): lax.all_gather(image_rows, 'band', axis=0, tiled=True)  116 us
    unnamed x1, blocking collectives  113 us
    psum x1, blocking collectives, on_device(): lax.psum((margin_rows, image_rows, local_norms), 'grid')  62.3 us
    ppermute x5, waiting for transfers between devices, padded_2(): lax.ppermute(tail, axis, [(i, (i + 1) % count) for i in range(count)])  47.1 us
    ppermute x5, starting transfers between devices, padded_2(): lax.ppermute(head, axis, [((i + 1) % count, i) for i in range(count)])  27.6 us
    dot_general x1, matrix products, on_device(): jnp.dot(flat_bands, flat_piece.T, precision=lax.Precision.HIGHEST, prefer...  17 us
  transfers between devices with their start and end apart: 11, of which 5 were waited for; matrix products, arithmetic and copies ran while one was open for 3% of the time, Pallas kernels for 0%

commit v1 on v0

--- a/solution.py
+++ b/solution.py
@@ -10,6 +10,11 @@
 FOUR_THIRDS = 4.0 / 3.0
 TWELFTH = 1.0 / 12.0
 filter_degree = 4
+
+
+def exchange_gather(array, axis, d):
+    sent = jnp.stack([array] * lax.axis_size(axis))
+    return jnp.concatenate(lax.all_to_all(sent, axis, 0, 0), axis=d)
 
 
 def padded_2(cells, sides, width):
@@ -78,7 +83,7 @@
     margin_rows, image_rows, norm_rows = lax.psum((margin_rows, image_rows, local_norms), "grid")
     margin, subspace, image_norms = (
         lax.all_gather(margin_rows, "band", axis=0, tiled=True),
-        lax.all_gather(image_rows, "band", axis=0, tiled=True),
+        exchange_gather(image_rows, "band", 0),
         lax.all_gather(norm_rows, "band", axis=0, tiled=True),
     )
     margin = margin * inverse_cells

time: 829 us -> 733 us (0.88)
  blocking collectives: 409 us -> 298 us
  starting transfers between devices: 38.9 us -> 51.4 us
    all_gather x1 -> x0, blocking collectives: 116 us -> none  [on_device(): lax.all_gather(image_rows, 'band', axis=0, tiled=True)]
    all_to_all x0 -> x1, starting transfers between devices: none -> 12.6 us  [exchange_gather(): return jnp.concatenate(lax.all_to_all(sent, axis, 0, 0), axis=d)]
    unnamed x1, blocking collectives: 113 us -> 123 us
  transfers between devices with their start and end apart: 11 -> 12, of which waited for: 5 -> 5; matrix products, arithmetic and copies ran while one was open for 3% -> 5% of each run, Pallas kernels for 0% -> 0%
where the time goes in v1:
time: 733 us; the launch traced here: 731 us
  blocking collectives  298 us (41%)
  waiting for transfers between devices  289 us (39%)
  starting transfers between devices  51.4 us (7%)
  matrix products  30.3 us (4%)
  local copies, waits for them, and re-layouts  27.7 us (4%)
  other arithmetic  20.5 us (3%)
  between operations  15.1 us (2%)
    all_gather x1, waiting for transfers between devices, on_device(): panel_piece = lax.all_gather(current, 'band', axis=0, tiled=True)  242 us
    unnamed x1, blocking collectives  123 us
    all_gather x1, blocking collectives, on_device(): lax.all_gather(margin_rows, 'band', axis=0, tiled=True)  112 us
    psum x1, blocking collectives, on_device(): lax.psum((margin_rows, image_rows, local_norms), 'grid')  62.3 us
    ppermute x5, waiting for transfers between devices, padded_2(): lax.ppermute(tail, axis, [(i, (i + 1) % count) for i in range(count)])  47.1 us
    ppermute x5, starting transfers between devices, padded_2(): lax.ppermute(head, axis, [((i + 1) % count, i) for i in range(count)])  27.6 us
    dot_general x1, matrix products, on_device(): jnp.dot(flat_bands, flat_piece.T, precision=lax.Precision.HIGHEST, prefer...  17 us
  transfers between devices with their start and end apart: 12, of which 5 were waited for; matrix products, arithmetic and copies ran while one was open for 5% of the time, Pallas kernels for 0%

profile of v1, /device:TPU:32, one launch (start us, length us, event | category | flops | bytes accessed | tf_op | source)
XLA Modules:
  0.0 731.5 jit_solution(8606035640182124944)
XLA Ops:
  7.2 0.9 fusion.157
  8.1 1.9 collective-permute-start
  10.0 16.7 %collective-permute-start.1 = (f32[2,2,32,128]{3,2,1,0:T(8,128)S(1)}, f32[2,2,32,128]{3,2,1,0:T(8,128)S(1)}, u32[]{:S(2)}, u32[]{:S(2)}) collective-permute-start(f32[2,2,32,128]{3,2,1,0:T(8,128)S(1)} %get-tuple-element.100), channel_id=1, source_target_pairs={{1,0},{2,1},{3,2},{4,3},{5,4},{6,5},{7,6},{8,7},{9,8},{10,9},{11,1... | collective-permute-start | bytes 196616 | tf_op jit(solution)/shard_map/ppermute | solution.py:29
  26.8 1.2 fusion.160
  28.0 1.2 fusion.161
  29.2 0.9 fusion.158
  30.2 1.2 fusion.159
  31.4 1.3 fusion.155
  32.6 1.2 fusion.156
  33.9 1.2 fusion.154
  35.0 0.9 broadcast_multiply_fusion.1
  36.0 0.9 fusion.153
  36.9 1.0 constant_dynamic-update-slice_fusion
  38.0 1.7 broadcast_multiply_fusion
  40.0 0.2 fusion.149
  40.4 0.2 fusion.145
  40.6 5.1 collective-permute-start.3
  45.7 1.9 collective-permute-start.2
  47.6 14.4 %collective-permute-done.2 = f32[2,2,32,128]{3,2,1,0:T(8,128)S(1)} collective-permute-done((f32[2,2,32,128]{3,2,1,0:T(8,128)S(1)}, f32[2,2,32,128]{3,2,1,0:T(8,128)S(1)}, u32[]{:S(2)}, u32[]{:S(2)}) %collective-permute-start.2) | collective-permute-done | bytes 65568 | tf_op jit(solution)/shard_map/ppermute | solution.py:27
  62.1 0.7 fusion.65
  63.0 0.2 fusion.140
  63.5 0.2 fusion.136
  63.6 1.9 collective-permute-start.5
  65.5 2.4 collective-permute-start.4
  68.0 14.0 %collective-permute-done.4 = f32[2,2,32,128]{3,2,1,0:T(8,128)S(1)} collective-permute-done((f32[2,2,32,128]{3,2,1,0:T(8,128)S(1)}, f32[2,2,32,128]{3,2,1,0:T(8,128)S(1)}, u32[]{:S(2)}, u32[]{:S(2)}) %collective-permute-start.4) | collective-permute-done | bytes 65568 | tf_op jit(solution)/shard_map/ppermute | solution.py:27
  82.0 0.6 fusion.50
  82.9 0.2 fusion.131
  83.4 1.9 collective-permute-start.7
  85.4 2.4 collective-permute-start.6
  87.8 14.0 %collective-permute-done.6 = f32[2,2,32,128]{3,2,1,0:T(8,128)S(1)} collective-permute-done((f32[2,2,32,128]{3,2,1,0:T(8,128)S(1)}, f32[2,2,32,128]{3,2,1,0:T(8,128)S(1)}, u32[]{:S(2)}, u32[]{:S(2)}) %collective-permute-start.6) | collective-permute-done | bytes 65568 | tf_op jit(solution)/shard_map/ppermute | solution.py:27
  101.8 1.4 fusion.35
  103.2 1.3 dynamic-slice
  105.1 0.9 fusion.121
  106.0 1.9 collective-permute-start.9
  108.0 2.6 collective-permute-start.8
  110.6 0.9 fusion.122
  111.5 1.2 fusion.124
  112.7 1.2 fusion.125
  114.0 1.1 fusion.123
  115.1 1.2 fusion.119
  116.3 1.2 fusion.120
  117.6 1.1 fusion.118
  118.7 0.9 fusion.117
  119.7 4.7 collective-permute-done.8
  124.4 2.4 multiply_reduce_fusion
  126.8 241.7 %all-gather.3.cloned.1.call-done = f32[64,10,32,128]{3,2,1,0:T(8,128)} async-done(((f32[2,10,32,128]{3,2,1,0:T(8,128)}), f32[64,10,32,128]{3,2,1,0:T(8,128)}) %all-gather.3.cloned.1.call-update) | async-done | bytes 10485776 | tf_op jit(solution)/shard_map/all_gather | solution.py:67
  368.4 17.0 %fusion.4 = f32[2,64]{1,0:T(2,128)S(1)} fusion(f32[64,10,32,128]{3,2,1,0:T(8,128)} %all-gather.3.cloned.1.call-done, f32[2,10,32,128]{3,2,1,0:T(8,128)S(1)} %copy-done), kind=kOutput, calls=%fused_computation.4 | convolution fusion | flops 62914560 | bytes 10813952 | tf_op jit(solution)/shard_map/dot_general | solution.py:69
  385.5 12.8 %fusion.7 = f32[2,64]{1,0:T(2,128)S(1)} fusion(f32[64,10,32,128]{3,2,1,0:T(8,128)S(1)} %copy-done.2, f32[2,10,32,128]{3,2,1,0:T(8,128)S(1)} %get-tuple-element.14), kind=kOutput, calls=%fused_computation.5 | convolution fusion | flops 62914560 | bytes 10813952 | tf_op jit(solution)/shard_map/dot_general | solution.py:75
  398.3 62.3 %all-reduce.1 = (f32[2,64]{1,0:T(2,128)S(1)}, f32[2,64]{1,0:T(2,128)S(1)}, f32[2]{0:T(128)S(1)}) all-reduce(f32[2,64]{1,0:T(2,128)S(1)} %fusion.7, f32[2,64]{1,0:T(2,128)S(1)} %fusion.4, f32[2]{0:T(128)S(1)} %get-tuple-element.13), channel_id=1, replica_groups=mesh['band'=32,'grid'=16] {'grid'}, use_global_device_ids=true, to_apply=%region_3.4 | all-reduce | flops 258 | bytes 2064 | tf_op jit(solution)/shard_map/psum | solution.py:83
  460.6 0.7 reshape.44
  461.3 12.6 %all-to-all-start = ((f32[32,1,128]{2,1,0:T(1,128)}), f32[32,1,128]{2,1,0:T(1,128)S(1)}, u32[]{:S(2)}, u32[]{:S(2)}) async-start(f32[32,1,128]{2,1,0:T(1,128)} %reshape.44), calls=%async_computation | async-start | bytes 32768 | tf_op jit(solution)/shard_map/all_to_all | solution.py:17
  473.9 112.0 %all-gather = f32[32,2,64]{2,1,0:T(2,128)S(1)} all-gather(f32[1,2,64]{2,1,0:T(2,128)S(1)} %bitcast.36), channel_id=1, replica_groups=mesh['band'=32,'grid'=16] {'band'}, dimensions={0}, use_global_device_ids=true | all-gather | bytes 16896 | tf_op jit(solution)/shard_map/all_gather | solution.py:85
  586.0 5.8 cholesky.18
  591.8 0.6 compare_reduce_fusion
  592.5 0.7 fusion.108
  593.1 4.9 custom-call.8
  598.1 0.2 dynamic-update-slice.3
  598.3 123.3 %all-reduce = f32[64]{0:T(128)S(1)} all-reduce(f32[64]{0:T(128)S(1)} %dynamic-update-slice.3), channel_id=1, replica_groups=mesh['band'=32,'grid'=16] {'band'}, use_global_device_ids=true, to_apply=%add | all-reduce | flops 64 | bytes 512
  721.6 0.5 broadcast.119
  722.1 0.7 reduce.7
  723.0 0.3 multiply_reduce_fusion.1
  723.2 0.2 fusion.109
  723.5 0.6 constant_dynamic-slice_fusion
  724.0 0.6 dynamic_slice.7
  (50 shorter events, 2.0 us)
Async XLA Ops:
  7.2 361.3 %all-gather.3.cloned.1.call-start = ((), (), s32[]{:S(2)}) async-start(), calls=%async_computation.1 | async-start | bytes 10813440 | tf_op jit(solution)/shard_map/all_gather | solution.py:67
  8.1 28.8 %collective-permute-start = (f32[2,2,32,128]{3,2,1,0:T(8,128)S(1)}, f32[2,2,32,128]{3,2,1,0:T(8,128)S(1)}, u32[]{:S(2)}, u32[]{:S(2)}) collective-permute-start(f32[2,2,32,128]{3,2,1,0:T(8,128)S(1)} %get-tuple-element.99), channel_id=1, source_target_pairs={{0,1},{1,2},{2,3},{3,4},{4,5},{5,6},{6,7},{7,8},{8,9},{9,10},{10,1... | collective-permute-start | bytes 196616 | tf_op jit(solution)/shard_map/ppermute | solution.py:27
  10.0 28.0 %collective-permute-start.1 = (f32[2,2,32,128]{3,2,1,0:T(8,128)S(1)}, f32[2,2,32,128]{3,2,1,0:T(8,128)S(1)}, u32[]{:S(2)}, u32[]{:S(2)}) collective-permute-start(f32[2,2,32,128]{3,2,1,0:T(8,128)S(1)} %get-tuple-element.100), channel_id=1, source_target_pairs={{1,0},{2,1},{3,2},{4,3},{5,4},{6,5},{7,6},{8,7},{9,8},{10,9},{11,1... | collective-permute-start | bytes 196616 | tf_op jit(solution)/shard_map/ppermute | solution.py:29
  31.3 30.8 %copy-start.1 = (f32[2,10,32,128]{3,2,1,0:T(8,128)S(1)}, f32[2,10,32,128]{3,2,1,0:T(8,128)}, u32[]{:S(2)}) copy-start(f32[2,10,32,128]{3,2,1,0:T(8,128)} %param.4) | copy-start | bytes 983044
  39.8 42.2 %copy-start.3 = (f32[10,32,128]{2,1,0:T(8,128)S(1)}, f32[10,32,128]{2,1,0:T(8,128)}, u32[]{:S(2)}) copy-start(f32[10,32,128]{2,1,0:T(8,128)} %param.5) | copy-start | bytes 491524
  40.6 7.1 collective-permute-start.3
  45.7 16.4 %collective-permute-start.2 = (f32[2,2,32,128]{3,2,1,0:T(8,128)S(1)}, f32[2,2,32,128]{3,2,1,0:T(8,128)S(1)}, u32[]{:S(2)}, u32[]{:S(2)}) collective-permute-start(f32[2,2,32,128]{3,2,1,0:T(8,128)S(1)} %get-tuple-element.87), channel_id=1, source_target_pairs={{0,1},{1,2},{2,3},{3,4},{4,5},{5,6},{6,7},{7,8},{8,9},{9,10},{10,1... | collective-permute-start | bytes 196616 | tf_op jit(solution)/shard_map/ppermute | solution.py:27
  63.6 4.4 collective-permute-start.5
  65.5 16.4 %collective-permute-start.4 = (f32[2,2,32,128]{3,2,1,0:T(8,128)S(1)}, f32[2,2,32,128]{3,2,1,0:T(8,128)S(1)}, u32[]{:S(2)}, u32[]{:S(2)}) collective-permute-start(f32[2,2,32,128]{3,2,1,0:T(8,128)S(1)} %get-tuple-element.69), channel_id=1, source_target_pairs={{0,1},{1,2},{2,3},{3,4},{4,5},{5,6},{6,7},{7,8},{8,9},{9,10},{10,1... | collective-permute-start | bytes 196616 | tf_op jit(solution)/shard_map/ppermute | solution.py:27
  83.4 4.4 collective-permute-start.7
  85.4 16.4 %collective-permute-start.6 = (f32[2,2,32,128]{3,2,1,0:T(8,128)S(1)}, f32[2,2,32,128]{3,2,1,0:T(8,128)S(1)}, u32[]{:S(2)}, u32[]{:S(2)}) collective-permute-start(f32[2,2,32,128]{3,2,1,0:T(8,128)S(1)} %get-tuple-element.51), channel_id=1, source_target_pairs={{0,1},{1,2},{2,3},{3,4},{4,5},{5,6},{6,7},{7,8},{8,9},{9,10},{10,1... | collective-permute-start | bytes 196616 | tf_op jit(solution)/shard_map/ppermute | solution.py:27
  103.2 265.3 %copy-start = (f32[2,10,32,128]{3,2,1,0:T(8,128)S(1)}, f32[2,10,32,128]{3,2,1,0:T(8,128)}, u32[]{:S(2)}) copy-start(f32[2,10,32,128]{3,2,1,0:T(8,128)} %fusion.35) | copy-start | bytes 983044
  106.0 13.6 %collective-permute-start.9 = (f32[2,2,32,128]{3,2,1,0:T(8,128)S(1)}, f32[2,2,32,128]{3,2,1,0:T(8,128)S(1)}, u32[]{:S(2)}, u32[]{:S(2)}) collective-permute-start(f32[2,2,32,128]{3,2,1,0:T(8,128)S(1)} %get-tuple-element.26), channel_id=1, source_target_pairs={{1,0},{2,1},{3,2},{4,3},{5,4},{6,5},{7,6},{8,7},{9,8},{10,9},{11,1... | collective-permute-start | bytes 196616 | tf_op jit(solution)/shard_map/ppermute | solution.py:29
  108.0 16.4 %collective-permute-start.8 = (f32[2,2,32,128]{3,2,1,0:T(8,128)S(1)}, f32[2,2,32,128]{3,2,1,0:T(8,128)S(1)}, u32[]{:S(2)}, u32[]{:S(2)}) collective-permute-start(f32[2,2,32,128]{3,2,1,0:T(8,128)S(1)} %get-tuple-element.25), channel_id=1, source_target_pairs={{0,1},{1,2},{2,3},{3,4},{4,5},{5,6},{6,7},{7,8},{8,9},{9,10},{10,1... | collective-permute-start | bytes 196616 | tf_op jit(solution)/shard_map/ppermute | solution.py:27
  368.4 17.0 %copy-start.2 = (f32[64,10,32,128]{3,2,1,0:T(8,128)S(1)}, f32[64,10,32,128]{3,2,1,0:T(8,128)}, u32[]{:S(2)}) copy-start(f32[64,10,32,128]{3,2,1,0:T(8,128)} %all-gather.3.cloned.1.call-done) | copy-start | bytes 31457284
  461.3 260.4 %all-to-all-start = ((f32[32,1,128]{2,1,0:T(1,128)}), f32[32,1,128]{2,1,0:T(1,128)S(1)}, u32[]{:S(2)}, u32[]{:S(2)}) async-start(f32[32,1,128]{2,1,0:T(1,128)} %reshape.44), calls=%async_computation | async-start | bytes 32768 | tf_op jit(solution)/shard_map/all_to_all | solution.py:17
Sparse Core Ops, SparseCore 0:
  103.3 265.0 all-gather.2
